TPU v7x, 32 devices: a whole 2x2x4 slice. The times are simulated.
32 devices in a mesh: tok: 8 (over z, core), head: 4 (over y, x).
Axes of the slice: x: 2, y: 2, z: 4, core: 2. Of those that a mesh axis runs over, the one named last changes fastest.
Arguments:
- query_states: bfloat16 [12288, 3072], P('tok', 'head')
- key_states: bfloat16 [12288, 3072], P('tok', 'head')
- value_states: bfloat16 [12288, 3072], P('tok', 'head'), may hold values from -6 to 6
- query_gain: float32 [3072], P('head'), may hold values from 1 to 2.5
- key_gain: float32 [3072], P('head'), may hold values from 1 to 2.5
- windows: int32 [48, 27], P('tok'), may hold values from -1 to 47, as said below
Outputs:
- attention: bfloat16 [12288, 3072], P('tok', 'head')
Inputs may be any that keep to these rules, and one draw needn't show every extreme that they name: Slots 0 to 8 of windows[i] name tiles of the tile-frame before tile i's, the next 9 tiles of its own tile-frame, the last 9 tiles of the tile-frame after it; in each group the named tiles come first and -1 fills the rest; tile i itself is always named; no tile is named twice in a row; a named tile's tile row and tile column differ from tile i's by at most 2 each, and some named tiles differ by 2 in both.
All inputs are finite; a program needn't handle non-finite values.
Results may differ from a plain program's by a relative error of at most 0.012.
The roundings to bfloat16 on the way count: a program that leaves them out, or rounds other values in their place, can miss the bound.
Values may be sent and summed in bfloat16 or wider, within the bound.
No kernel may reach another device: no remote copies, remote signals or barrier semaphores. Data moves between devices by JAX's collectives and lax.ppermute only.
A program may use at most 320 MiB of HBM per device.

v0:
```python
import math

import jax
import jax.numpy as jnp
from jax import lax
from jax.experimental import pallas as pl
from jax.experimental.pallas import tpu as pltpu
from jax.sharding import PartitionSpec as P

HEAD_DIM = 128
MODEL_DIM = 3072
TILE_TOKENS = 256
WINDOW_SLOTS = 27


def square_sums(source):
    widened = source.astype(jnp.float32)
    return jnp.sum(widened * widened, axis=1)


def normalize_rows(source, totals, scale_gain):
    widened = source.astype(jnp.float32)
    return (widened * lax.rsqrt(totals[:, None] / MODEL_DIM + 1e-06) * scale_gain).astype(
        jnp.bfloat16
    )


def compact_windows(windows, tile_count):
    valid = windows >= 0
    order = jnp.argsort(jnp.logical_not(valid).astype(jnp.int32), axis=1, stable=True)
    ids = jnp.take_along_axis(windows, order, axis=1)
    counts = jnp.sum(valid.astype(jnp.int32), axis=1)
    last = jnp.take_along_axis(ids, jnp.maximum(counts - 1, 0)[:, None], axis=1)
    slot = lax.broadcasted_iota(jnp.int32, ids.shape, 1)
    ids = jnp.where(slot < counts[:, None], ids, last)
    ids = jnp.clip(ids, 0, tile_count - 1)
    return ids.reshape(-1).astype(jnp.int32), counts.astype(jnp.int32)


def attention_kernel(ids_ref, cnt_ref, q_ref, k_ref, v_ref, o_ref, m_sc, l_sc, acc_sc):
    t = pl.program_id(0)
    s = pl.program_id(1)
    heads = q_ref.shape[1] // HEAD_DIM
    score_scale = 1.0 / math.sqrt(HEAD_DIM)

    @pl.when(s == 0)
    def _init():
        m_sc[...] = jnp.full(m_sc.shape, -jnp.inf, jnp.float32)
        l_sc[...] = jnp.zeros(l_sc.shape, jnp.float32)
        acc_sc[...] = jnp.zeros(acc_sc.shape, jnp.float32)

    @pl.when(s < cnt_ref[t])
    def _step():
        for h in range(heads):
            cols = slice(h * HEAD_DIM, (h + 1) * HEAD_DIM)
            q = q_ref[:, cols]
            k = k_ref[0, :, cols]
            v = v_ref[0, :, cols]
            scores = (
                lax.dot_general(
                    q, k, (((1,), (1,)), ((), ())), preferred_element_type=jnp.float32
                )
                * score_scale
            )
            m_prev = m_sc[h]
            m_cur = jnp.max(scores, axis=1, keepdims=True)
            m_new = jnp.maximum(m_prev, m_cur)
            alpha = jnp.exp(m_prev - m_new)
            weights = jnp.exp(scores - m_new[:, :1])
            l_sc[h] = alpha * l_sc[h] + jnp.sum(weights, axis=1, keepdims=True)
            m_sc[h] = m_new
            mixed = jnp.dot(
                weights.astype(jnp.bfloat16), v, preferred_element_type=jnp.float32
            )
            acc_sc[:, cols] = acc_sc[:, cols] * alpha + mixed

    @pl.when(s == pl.num_programs(1) - 1)
    def _finish():
        for h in range(heads):
            cols = slice(h * HEAD_DIM, (h + 1) * HEAD_DIM)
            o_ref[:, cols] = (acc_sc[:, cols] / l_sc[h]).astype(o_ref.dtype)


def window_attention(query_normed, keys, key_lead, values, value_lead, ids, counts, offset, group_width, previous):
    rows, width = query_normed.shape
    local_tiles = rows // TILE_TOKENS
    heads = group_width // HEAD_DIM
    group = offset // group_width
    in_specs = [
        pl.BlockSpec((TILE_TOKENS, group_width), lambda t, s, ids, cnt: (t, group)),
        pl.BlockSpec(
            (1, TILE_TOKENS, group_width),
            lambda t, s, ids, cnt: (key_lead, ids[t * WINDOW_SLOTS + s], 0),
        ),
        pl.BlockSpec(
            (1, TILE_TOKENS, group_width),
            lambda t, s, ids, cnt: (value_lead, ids[t * WINDOW_SLOTS + s], 0),
        ),
    ]
    operands = [ids, counts, query_normed, keys, values]
    aliases = {}
    kernel = attention_kernel
    if previous is not None:
        in_specs.append(pl.BlockSpec(memory_space=pl.ANY))
        operands.append(previous)
        aliases = {5: 0}

        def kernel(ids_ref, cnt_ref, q_ref, k_ref, v_ref, prev_ref, o_ref, m_sc, l_sc, acc_sc):
            attention_kernel(ids_ref, cnt_ref, q_ref, k_ref, v_ref, o_ref, m_sc, l_sc, acc_sc)

    grid_spec = pltpu.PrefetchScalarGridSpec(
        num_scalar_prefetch=2,
        grid=(local_tiles, WINDOW_SLOTS),
        in_specs=in_specs,
        out_specs=pl.BlockSpec((TILE_TOKENS, group_width), lambda t, s, ids, cnt: (t, group)),
        scratch_shapes=[
            pltpu.VMEM((heads, TILE_TOKENS, HEAD_DIM), jnp.float32),
            pltpu.VMEM((heads, TILE_TOKENS, HEAD_DIM), jnp.float32),
            pltpu.VMEM((TILE_TOKENS, group_width), jnp.float32),
        ],
    )
    return pl.pallas_call(
        kernel,
        grid_spec=grid_spec,
        out_shape=jax.ShapeDtypeStruct((rows, width), jnp.bfloat16),
        input_output_aliases=aliases,
        compiler_params=pltpu.CompilerParams(
            dimension_semantics=("arbitrary", "arbitrary")
        ),
    )(*operands)


def head_groups(heads_here):
    if heads_here % 2 == 0 and heads_here >= 4:
        return [2] * (heads_here // 2 - 1) + [1, 1]
    return [1] * heads_here


def on_device(query_states, key_states, value_states, query_gain, key_gain, windows):
    sizes = head_groups(query_states.shape[1] // HEAD_DIM)
    offsets = [HEAD_DIM * sum(sizes[:number]) for number in range(len(sizes))]
    widths = [HEAD_DIM * size for size in sizes]

    def columns(source, number):
        return source[:, offsets[number]:offsets[number] + widths[number]]

    query_total, key_total = lax.psum((square_sums(query_states), square_sums(key_states)), "head")
    query_normed = normalize_rows(query_states, query_total, query_gain)
    sent_keys = normalize_rows(key_states, key_total, key_gain)
    tile_count = query_states.shape[0] * lax.psum(1, "tok") // TILE_TOKENS
    ids, counts = compact_windows(windows, tile_count)
    output = None
    for number in range(len(sizes)):
        paired = jnp.stack([columns(sent_keys, number), columns(value_states, number)])
        extended = lax.all_gather(paired, "tok", axis=1, tiled=True)
        output = window_attention(
            query_normed, extended, 0, extended, 1, ids, counts,
            offsets[number], widths[number], output,
        )
    return output


def solution(mesh):
    in_specs = (
        P("tok", "head"),
        P("tok", "head"),
        P("tok", "head"),
        P("head"),
        P("head"),
        P("tok", None),
    )
    out_specs = P("tok", "head")
    return jax.shard_map(
        on_device, mesh=mesh, in_specs=in_specs, out_specs=out_specs, check_vma=False
    )
```

profile of v0, /device:TPU:11, one launch (start us, length us, event | category | flops | bytes accessed | tf_op | source)
XLA Modules:
  0.0 608.6 jit_solution(11457307377461670144)
XLA Ops:
  6.5 0.0 copy-start.1
  6.5 0.0 copy-start.6
  6.5 0.0 all-gather.11.cloned.1.call-start
  6.5 3.5 fusion
  10.1 10.6 %all-reduce = (f32[1536]{0:T(1024)S(1)}, f32[1536]{0:T(1024)S(1)}) all-reduce(f32[1536]{0:T(1024)S(1)} %get-tuple-element.19, f32[1536]{0:T(1024)S(1)} %get-tuple-element.20), channel_id=1, replica_groups=mesh['tok'=8,'head'=4] {'head'}, use_global_device_ids=true, to_apply=%region_3.0 | all-reduce | flops 3072 | bytes 24576 | tf_op jit(solution)/shard_map/psum | solution.py:147
  20.7 0.0 copy-done.1
  20.7 0.0 copy-done.6
  20.7 0.6 fusion.5
  21.3 0.0 copy-start.3
  21.3 0.0 copy-start.4
  21.3 0.1 slice_bitcast_fusion
  21.4 2.4 copy-done.4
  23.8 0.1 slice_bitcast_fusion.2
  23.9 0.0 copy-done.3
  23.9 1.3 pad_maximum_fusion.1
  25.2 0.0 all-gather.11.cloned.1.call-update
  25.3 0.0 all-gather.9.cloned.1.call-start
  25.3 1.3 pad_maximum_fusion
  26.6 0.0 all-gather.9.cloned.1.call-update
  26.6 0.0 all-gather.7.cloned.1.call-start
  26.6 1.2 slice_bitcast_fusion.4
  27.8 1.2 slice_bitcast_fusion.6
  29.0 0.0 copy-start
  29.0 0.9 pad_maximum_fusion.3
  30.0 0.0 all-gather.7.cloned.1.call-update
  30.0 0.0 all-gather.5.cloned.1.call-start
  30.0 1.0 pad_maximum_fusion.2
  31.0 0.0 all-gather.5.cloned.1.call-update
  31.0 0.0 copy-done
  31.1 0.1 convert_reduce_fusion
  31.2 0.1 copy.10
  31.3 0.8 sort.17
  32.1 0.1 copy.11
  32.2 0.1 reshape.73
  32.3 1.7 gather_fusion
  34.0 0.1 reshape.76
  34.1 0.6 gather_fusion.1
  34.7 0.0 copy-done.5
  34.8 0.1 select_clamp_fusion
  34.8 0.7 min.12.ids_ref
  35.5 0.0 copy-done.2
  35.5 0.0 copy-done.7
  35.5 2.0 fusion.2.q_ref
  37.5 107.1 %all-gather.11.cloned.1.call-done.k_ref.v_ref = bf16[2,12288,256]{2,1,0:T(8,128)(2,1)} async-done(((bf16[2,1536,256]{2,1,0:T(8,128)(2,1)}), bf16[2,12288,256]{2,1,0:T(8,128)(2,1)}) %all-gather.11.cloned.1.call-update) | async-done | bytes 12582928 | tf_op jit(solution)/shard_map/all_gather | solution.py:155
  144.5 131.4 %shard_map.64.prev_ref = bf16[1536,768]{1,0:T(8,128)(2,1)} custom-call(s32[162]{0:T(256)} %min.12.ids_ref, s32[6]{0:T(128)} %copy-done.5, bf16[1536,768]{1,0:T(8,128)(2,1)} %fusion.2.q_ref, bf16[2,12288,256]{2,1,0:T(8,128)(2,1)} %all-gather.11.cloned.1.call-done.k_ref.v_ref, bf16[2,12288,256]{2,1,0:T(8,128)(2,1)} %all-gather.11.cloned.1.call-done.k_ref.v_ref), custom_call_target="tpu_custom_call" | custom-call | tf_op jit(solution)/shard_map/pallas_call | solution.py:122
  275.9 132.0 %shard_map.65.prev_ref = bf16[1536,768]{1,0:T(8,128)(2,1)} custom-call(s32[162]{0:T(256)} %min.12.ids_ref, s32[6]{0:T(128)} %copy-done.5, bf16[1536,768]{1,0:T(8,128)(2,1)} %fusion.2.q_ref, bf16[2,12288,256]{2,1,0:T(8,128)(2,1)} %all-gather.9.cloned.1.call-done.k_ref.v_ref, ...), custom_call_target="tpu_custom_call", output_to_operand_aliasing={{}: (5, {})} | custom-call | tf_op jit(solution)/shard_map/pallas_call | solution.py:122
  407.9 97.1 %shard_map.66.prev_ref = bf16[1536,768]{1,0:T(8,128)(2,1)} custom-call(s32[162]{0:T(256)} %min.12.ids_ref, s32[6]{0:T(128)} %copy-done.5, bf16[1536,768]{1,0:T(8,128)(2,1)} %fusion.2.q_ref, bf16[2,12288,128]{2,1,0:T(8,128)(2,1)} %all-gather.7.cloned.1.call-done.k_ref.v_ref, ...), custom_call_target="tpu_custom_call", output_to_operand_aliasing={{}: (5, {})} | custom-call | tf_op jit(solution)/shard_map/pallas_call | solution.py:122
  505.0 97.1 %shard_map.67 = bf16[1536,768]{1,0:T(8,128)(2,1)} custom-call(s32[162]{0:T(256)} %min.12.ids_ref, s32[6]{0:T(128)} %copy-done.5, bf16[1536,768]{1,0:T(8,128)(2,1)} %fusion.2.q_ref, bf16[2,12288,128]{2,1,0:T(8,128)(2,1)} %all-gather.5.cloned.1.call-done.k_ref.v_ref, ...), custom_call_target="tpu_custom_call", output_to_operand_aliasing={{}: (5, {})} | custom-call | tf_op jit(solution)/shard_map/pallas_call | solution.py:122
  (17 shorter events, 0.1 us)
Async XLA Ops:
  6.5 14.1 %copy-start.1 = (bf16[1536,768]{1,0:T(8,128)(2,1)S(1)}, bf16[1536,768]{1,0:T(8,128)(2,1)}, u32[]{:S(2)}) copy-start(bf16[1536,768]{1,0:T(8,128)(2,1)} %param.7) | copy-start | bytes 7077892
  6.5 14.1 %copy-start.6 = (f32[768]{0:T(1024)S(1)}, f32[768]{0:T(1024)}, u32[]{:S(2)}) copy-start(f32[768]{0:T(1024)} %param.10) | copy-start | bytes 9220
  6.5 138.0 %all-gather.11.cloned.1.call-start = ((), (), s32[]{:S(2)}) async-start(), calls=%async_computation.3 | async-start | bytes 14155776 | tf_op jit(solution)/shard_map/all_gather | solution.py:155
  21.3 2.6 copy-start.3
  21.3 2.5 copy-start.4
  25.3 250.7 %all-gather.9.cloned.1.call-start = ((), (), s32[]{:S(2)}) async-start(), calls=%async_computation.2 | async-start | bytes 14155776 | tf_op jit(solution)/shard_map/all_gather | solution.py:155
  26.6 381.4 %all-gather.7.cloned.1.call-start = ((), (), s32[]{:S(2)}) async-start(), calls=%async_computation.1 | async-start | bytes 7077888 | tf_op jit(solution)/shard_map/all_gather | solution.py:155
  29.0 2.0 copy-start
  30.0 475.0 %all-gather.5.cloned.1.call-start = ((), (), s32[]{:S(2)}) async-start(), calls=%async_computation | async-start | bytes 7077888 | tf_op jit(solution)/shard_map/all_gather | solution.py:155
  31.2 3.6 copy-start.5
  32.3 3.2 copy-start.2
  32.3 3.2 copy-start.7
Sparse Core Ops, SparseCore 0:
  25.4 119.1 all-gather.10
  146.1 114.9 all-gather.8
  262.7 63.4 all-gather.6
  327.7 63.4 all-gather.4
where the time goes:
time: 619 us; the launch traced here: 609 us
  Pallas kernels  457 us (74%)
  waiting for transfers between devices  107 us (17%)
  between operations  13.3 us (2%)
  other arithmetic  11.7 us (2%)
  blocking collectives  10.6 us (2%)
  local copies, waits for them, and re-layouts  8.31 us (1%)
    pallas_call x4, Pallas kernels, window_attention(): pl.pallas_call(kernel, grid_spec=grid_spec, out_shape=jax.ShapeDtypeStruc...  457 us
    all_gather x4, waiting for transfers between devices, on_device(): extended = lax.all_gather(paired, 'tok', axis=1, tiled=True)  107 us
  transfers between devices with their start and end apart: 4, of which 1 were waited for; matrix products, arithmetic and copies ran while one was open for 2% of the time, Pallas kernels for 59%

commit v1 on v0

--- a/solution.py
+++ b/solution.py
@@ -11,6 +11,7 @@
 MODEL_DIM = 3072
 TILE_TOKENS = 256
 WINDOW_SLOTS = 27
+SLOTS_PER_STEP = 3
 
 
 def square_sums(source):
@@ -37,44 +38,51 @@
     return ids.reshape(-1).astype(jnp.int32), counts.astype(jnp.int32)
 
 
-def attention_kernel(ids_ref, cnt_ref, q_ref, k_ref, v_ref, o_ref, m_sc, l_sc, acc_sc):
+def attention_kernel(ids_ref, cnt_ref, q_ref, *refs):
+    k_refs = refs[:SLOTS_PER_STEP]
+    v_refs = refs[SLOTS_PER_STEP:2 * SLOTS_PER_STEP]
+    o_ref, m_sc, l_sc, acc_sc = refs[-4:]
     t = pl.program_id(0)
-    s = pl.program_id(1)
+    j = pl.program_id(1)
     heads = q_ref.shape[1] // HEAD_DIM
     score_scale = 1.0 / math.sqrt(HEAD_DIM)
 
-    @pl.when(s == 0)
+    @pl.when(j == 0)
     def _init():
         m_sc[...] = jnp.full(m_sc.shape, -jnp.inf, jnp.float32)
         l_sc[...] = jnp.zeros(l_sc.shape, jnp.float32)
         acc_sc[...] = jnp.zeros(acc_sc.shape, jnp.float32)
 
-    @pl.when(s < cnt_ref[t])
-    def _step():
-        for h in range(heads):
-            cols = slice(h * HEAD_DIM, (h + 1) * HEAD_DIM)
-            q = q_ref[:, cols]
-            k = k_ref[0, :, cols]
-            v = v_ref[0, :, cols]
-            scores = (
-                lax.dot_general(
-                    q, k, (((1,), (1,)), ((), ())), preferred_element_type=jnp.float32
+    for sub in range(SLOTS_PER_STEP):
+        k_ref = k_refs[sub]
+        v_ref = v_refs[sub]
+
+        @pl.when(j * SLOTS_PER_STEP + sub < cnt_ref[t])
+        def _step():
+            for h in range(heads):
+                cols = slice(h * HEAD_DIM, (h + 1) * HEAD_DIM)
+                q = q_ref[:, cols]
+                k = k_ref[0, :, cols]
+                v = v_ref[0, :, cols]
+                scores = (
+                    lax.dot_general(
+                        q, k, (((1,), (1,)), ((), ())), preferred_element_type=jnp.float32
+                    )
+                    * score_scale
                 )
-                * score_scale
-            )
-            m_prev = m_sc[h]
-            m_cur = jnp.max(scores, axis=1, keepdims=True)
-            m_new = jnp.maximum(m_prev, m_cur)
-            alpha = jnp.exp(m_prev - m_new)
-            weights = jnp.exp(scores - m_new[:, :1])
-            l_sc[h] = alpha * l_sc[h] + jnp.sum(weights, axis=1, keepdims=True)
-            m_sc[h] = m_new
-            mixed = jnp.dot(
-                weights.astype(jnp.bfloat16), v, preferred_element_type=jnp.float32
-            )
-            acc_sc[:, cols] = acc_sc[:, cols] * alpha + mixed
+                m_prev = m_sc[h]
+                m_cur = jnp.max(scores, axis=1, keepdims=True)
+                m_new = jnp.maximum(m_prev, m_cur)
+                alpha = jnp.exp(m_prev - m_new)
+                weights = jnp.exp(scores - m_new[:, :1])
+                l_sc[h] = alpha * l_sc[h] + jnp.sum(weights, axis=1, keepdims=True)
+                m_sc[h] = m_new
+                mixed = jnp.dot(
+                    weights.astype(jnp.bfloat16), v, preferred_element_type=jnp.float32
+                )
+                acc_sc[:, cols] = acc_sc[:, cols] * alpha + mixed
 
-    @pl.when(s == pl.num_programs(1) - 1)
+    @pl.when(j == pl.num_programs(1) - 1)
     def _finish():
         for h in range(heads):
             cols = slice(h * HEAD_DIM, (h + 1) * HEAD_DIM)
@@ -86,33 +94,34 @@
     local_tiles = rows // TILE_TOKENS
     heads = group_width // HEAD_DIM
     group = offset // group_width
-    in_specs = [
-        pl.BlockSpec((TILE_TOKENS, group_width), lambda t, s, ids, cnt: (t, group)),
-        pl.BlockSpec(
+    steps = WINDOW_SLOTS // SLOTS_PER_STEP
+
+    def window_spec(lead, sub):
+        return pl.BlockSpec(
             (1, TILE_TOKENS, group_width),
-            lambda t, s, ids, cnt: (key_lead, ids[t * WINDOW_SLOTS + s], 0),
-        ),
-        pl.BlockSpec(
-            (1, TILE_TOKENS, group_width),
-            lambda t, s, ids, cnt: (value_lead, ids[t * WINDOW_SLOTS + s], 0),
-        ),
-    ]
-    operands = [ids, counts, query_normed, keys, values]
+            lambda t, j, ids, cnt: (lead, ids[t * WINDOW_SLOTS + j * SLOTS_PER_STEP + sub], 0),
+        )
+
+    in_specs = [pl.BlockSpec((TILE_TOKENS, group_width), lambda t, j, ids, cnt: (t, group))]
+    in_specs += [window_spec(key_lead, sub) for sub in range(SLOTS_PER_STEP)]
+    in_specs += [window_spec(value_lead, sub) for sub in range(SLOTS_PER_STEP)]
+    operands = [ids, counts, query_normed]
+    operands += [keys] * SLOTS_PER_STEP + [values] * SLOTS_PER_STEP
     aliases = {}
     kernel = attention_kernel
     if previous is not None:
         in_specs.append(pl.BlockSpec(memory_space=pl.ANY))
+        aliases = {len(operands): 0}
         operands.append(previous)
-        aliases = {5: 0}
 
-        def kernel(ids_ref, cnt_ref, q_ref, k_ref, v_ref, prev_ref, o_ref, m_sc, l_sc, acc_sc):
-            attention_kernel(ids_ref, cnt_ref, q_ref, k_ref, v_ref, o_ref, m_sc, l_sc, acc_sc)
+        def kernel(ids_ref, cnt_ref, q_ref, *refs):
+            attention_kernel(ids_ref, cnt_ref, q_ref, *refs[:2 * SLOTS_PER_STEP], *refs[-4:])
 
     grid_spec = pltpu.PrefetchScalarGridSpec(
         num_scalar_prefetch=2,
-        grid=(local_tiles, WINDOW_SLOTS),
+        grid=(local_tiles, steps),
         in_specs=in_specs,
-        out_specs=pl.BlockSpec((TILE_TOKENS, group_width), lambda t, s, ids, cnt: (t, group)),
+        out_specs=pl.BlockSpec((TILE_TOKENS, group_width), lambda t, j, ids, cnt: (t, group)),
         scratch_shapes=[
             pltpu.VMEM((heads, TILE_TOKENS, HEAD_DIM), jnp.float32),
             pltpu.VMEM((heads, TILE_TOKENS, HEAD_DIM), jnp.float32),

time: 619 us -> 589 us (0.952); the launches traced: 609 us -> 597 us
  Pallas kernels: 457 us -> 446 us
    pallas_call x4, Pallas kernels: 457 us -> 446 us  [window_attention(): pl.pallas_call(kernel, grid_spec=grid_spec, out_shape=jax.ShapeDtypeStruc...]
  transfers between devices with their start and end apart: 4 -> 4, of which waited for: 1 -> 1; matrix products, arithmetic and copies ran while one was open for 2% -> 2% of each run, Pallas kernels for 59% -> 61%
where the time goes in v1:
time: 589 us; the launch traced here: 597 us
  Pallas kernels  446 us (76%)
  waiting for transfers between devices  107 us (18%)
  between operations  13.3 us (2%)
  other arithmetic  11.7 us (2%)
  blocking collectives  10.6 us (2%)
  local copies, waits for them, and re-layouts  8.31 us (1%)
    pallas_call x4, Pallas kernels, window_attention(): pl.pallas_call(kernel, grid_spec=grid_spec, out_shape=jax.ShapeDtypeStruc...  446 us
    all_gather x4, waiting for transfers between devices, on_device(): extended = lax.all_gather(paired, 'tok', axis=1, tiled=True)  107 us
  transfers between devices with their start and end apart: 4, of which 1 were waited for; matrix products, arithmetic and copies ran while one was open for 2% of the time, Pallas kernels for 61%

profile of v1, /device:TPU:11, one launch (start us, length us, event | category | flops | bytes accessed | tf_op | source)
XLA Modules:
  0.0 597.1 jit_solution(14056378124940668954)
XLA Ops:
  6.5 0.0 copy-start.1
  6.5 0.0 copy-start.6
  6.5 0.0 all-gather.11.cloned.1.call-start
  6.5 3.5 fusion
  10.1 10.6 %all-reduce = (f32[1536]{0:T(1024)S(1)}, f32[1536]{0:T(1024)S(1)}) all-reduce(f32[1536]{0:T(1024)S(1)} %get-tuple-element.19, f32[1536]{0:T(1024)S(1)} %get-tuple-element.20), channel_id=1, replica_groups=mesh['tok'=8,'head'=4] {'head'}, use_global_device_ids=true, to_apply=%region_3.0 | all-reduce | flops 3072 | bytes 24576 | tf_op jit(solution)/shard_map/psum | solution.py:156
  20.7 0.0 copy-done.1
  20.7 0.0 copy-done.6
  20.7 0.6 fusion.5
  21.3 0.0 copy-start.3
  21.3 0.0 copy-start.4
  21.3 0.1 slice_bitcast_fusion
  21.4 2.4 copy-done.4
  23.8 0.1 slice_bitcast_fusion.2
  23.9 0.0 copy-done.3
  23.9 1.3 pad_maximum_fusion.1
  25.2 0.0 all-gather.11.cloned.1.call-update
  25.3 0.0 all-gather.9.cloned.1.call-start
  25.3 1.3 pad_maximum_fusion
  26.6 0.0 all-gather.9.cloned.1.call-update
  26.6 0.0 all-gather.7.cloned.1.call-start
  26.6 1.2 slice_bitcast_fusion.4
  27.8 1.2 slice_bitcast_fusion.6
  29.0 0.0 copy-start
  29.0 0.9 pad_maximum_fusion.3
  30.0 0.0 all-gather.7.cloned.1.call-update
  30.0 0.0 all-gather.5.cloned.1.call-start
  30.0 1.0 pad_maximum_fusion.2
  31.0 0.0 all-gather.5.cloned.1.call-update
  31.0 0.0 copy-done
  31.1 0.1 convert_reduce_fusion
  31.2 0.1 copy.10
  31.3 0.8 sort.17
  32.1 0.1 copy.11
  32.2 0.1 reshape.73
  32.3 1.7 gather_fusion
  34.0 0.1 reshape.76
  34.1 0.6 gather_fusion.1
  34.7 0.0 copy-done.5
  34.8 0.1 select_clamp_fusion
  34.8 0.7 min.12.ids_ref
  35.5 0.0 copy-done.2
  35.5 0.0 copy-done.7
  35.5 2.0 fusion.2.q_ref
  37.5 107.1 %all-gather.11.cloned.1.call-done.refs_0_.refs_1_.refs_2_.refs_3_.refs_4_.refs_5_ = bf16[2,12288,256]{2,1,0:T(8,128)(2,1)} async-done(((bf16[2,1536,256]{2,1,0:T(8,128)(2,1)}), bf16[2,12288,256]{2,1,0:T(8,128)(2,1)}) %all-gather.11.cloned.1.call-update) | async-done | bytes 12582928 | tf_op jit(solution)/shard_map/all_gather | solution.py:164
  144.5 138.4 %shard_map.64.refs_6_ = bf16[1536,768]{1,0:T(8,128)(2,1)} custom-call(s32[162]{0:T(256)} %min.12.ids_ref, s32[6]{0:T(128)} %copy-done.5, bf16[1536,768]{1,0:T(8,128)(2,1)} %fusion.2.q_ref, bf16[2,12288,256]{2,1,0:T(8,128)(2,1)} %all-gather.11.cloned.1.call-done.refs_0_.refs_1_.refs_2_.refs_3_.refs_4_.refs_5_, ...), custom_call_target="tpu_custom_call" | custom-call | tf_op jit(solution)/shard_map/pallas_call | solution.py:131
  283.0 138.4 %shard_map.65.refs_6_ = bf16[1536,768]{1,0:T(8,128)(2,1)} custom-call(s32[162]{0:T(256)} %min.12.ids_ref, s32[6]{0:T(128)} %copy-done.5, bf16[1536,768]{1,0:T(8,128)(2,1)} %fusion.2.q_ref, bf16[2,12288,256]{2,1,0:T(8,128)(2,1)} %all-gather.9.cloned.1.call-done.refs_0_.refs_1_.refs_2_.refs_3_.refs_4_.refs_5_, ...), custom_call_target="tpu_custom_call", output_to_operand_aliasing={{}: (9, {})} | custom-call | tf_op jit(solution)/shard_map/pallas_call | solution.py:131
  421.3 84.6 %shard_map.66.refs_6_ = bf16[1536,768]{1,0:T(8,128)(2,1)} custom-call(s32[162]{0:T(256)} %min.12.ids_ref, s32[6]{0:T(128)} %copy-done.5, bf16[1536,768]{1,0:T(8,128)(2,1)} %fusion.2.q_ref, bf16[2,12288,128]{2,1,0:T(8,128)(2,1)} %all-gather.7.cloned.1.call-done.refs_0_.refs_1_.refs_2_.refs_3_.refs_4_.refs_5_, ...), custom_call_target="tpu_custom_call", output_to_operand_aliasing={{}: (9, {})} | custom-call | tf_op jit(solution)/shard_map/pallas_call | solution.py:131
  505.9 84.6 %shard_map.67 = bf16[1536,768]{1,0:T(8,128)(2,1)} custom-call(s32[162]{0:T(256)} %min.12.ids_ref, s32[6]{0:T(128)} %copy-done.5, bf16[1536,768]{1,0:T(8,128)(2,1)} %fusion.2.q_ref, bf16[2,12288,128]{2,1,0:T(8,128)(2,1)} %all-gather.5.cloned.1.call-done.refs_0_.refs_1_.refs_2_.refs_3_.refs_4_.refs_5_, ...), custom_call_target="tpu_custom_call", output_to_operand_aliasing={{}: (9, {})} | custom-call | tf_op jit(solution)/shard_map/pallas_call | solution.py:131
  (17 shorter events, 0.1 us)
Async XLA Ops:
  6.5 14.1 %copy-start.1 = (bf16[1536,768]{1,0:T(8,128)(2,1)S(1)}, bf16[1536,768]{1,0:T(8,128)(2,1)}, u32[]{:S(2)}) copy-start(bf16[1536,768]{1,0:T(8,128)(2,1)} %param.7) | copy-start | bytes 7077892
  6.5 14.1 %copy-start.6 = (f32[768]{0:T(1024)S(1)}, f32[768]{0:T(1024)}, u32[]{:S(2)}) copy-start(f32[768]{0:T(1024)} %param.10) | copy-start | bytes 9220
  6.5 138.0 %all-gather.11.cloned.1.call-start = ((), (), s32[]{:S(2)}) async-start(), calls=%async_computation.3 | async-start | bytes 14155776 | tf_op jit(solution)/shard_map/all_gather | solution.py:164
  21.3 2.6 copy-start.3
  21.3 2.5 copy-start.4
  25.3 257.7 %all-gather.9.cloned.1.call-start = ((), (), s32[]{:S(2)}) async-start(), calls=%async_computation.2 | async-start | bytes 14155776 | tf_op jit(solution)/shard_map/all_gather | solution.py:164
  26.6 394.8 %all-gather.7.cloned.1.call-start = ((), (), s32[]{:S(2)}) async-start(), calls=%async_computation.1 | async-start | bytes 7077888 | tf_op jit(solution)/shard_map/all_gather | solution.py:164
  29.0 2.0 copy-start
  30.0 476.0 %all-gather.5.cloned.1.call-start = ((), (), s32[]{:S(2)}) async-start(), calls=%async_computation | async-start | bytes 7077888 | tf_op jit(solution)/shard_map/all_gather | solution.py:164
  31.2 3.6 copy-start.5
  32.3 3.2 copy-start.2
  32.3 3.2 copy-start.7
Sparse Core Ops, SparseCore 0:
  25.4 119.1 all-gather.10
  146.1 114.9 all-gather.8
  262.8 63.5 all-gather.6
  327.9 63.3 all-gather.4
